TPU v7x, 256 devices: a whole 4x4x8 slice. The times are simulated.
256 devices in a mesh: seq: 64 (over y, z, core), tr: 2 (over x_lo), tc: 2 (over x_hi).
Axes of the slice: x: 4 (x_hi: 2, x_lo: 2; x = x_hi * 2 + x_lo), y: 4, z: 8, core: 2. Of those that a mesh axis runs over, the one named last changes fastest.
Arguments:
- activations: bfloat16 [65536, 1024], P('seq', ('tr', 'tc')), may hold values from -6 to 6
- seg_len: int32 [64], P('seq'), may hold values from 1 to 1024, as said below
- seg_start: int32 [64], P('seq'), may hold values from 0 to 1, as said below
- memory_rates: float32 [3, 64, 8], P(None, 'seq'), may hold values from 0 to 1, as said below
- w_qkv: bfloat16 [1024, 3, 1024], P(None, None, ('tr', 'tc')), may hold values from -0.1875 to 0.1875
- conv_w: float32 [4, 3, 1024], P(None, None, ('tr', 'tc')), may hold values from -3 to 3
- persistent: bfloat16 [2, 16, 1024], P(None, None, ('tr', 'tc')), may hold values from -6 to 6
- w_out: bfloat16 [1024, 1024], P(('tr', 'tc')), may hold values from -0.1875 to 0.1875
- w_gate: bfloat16 [1024, 2816], P(None, ('tr', 'tc')), may hold values from -0.1875 to 0.1875
- w_up: bfloat16 [1024, 2816], P(None, ('tr', 'tc')), may hold values from -0.1875 to 0.1875
- w_down: bfloat16 [2816, 1024], P(('tr', 'tc')), may hold values from -0.109375 to 0.109375
Outputs:
- layer_out: bfloat16 [65536, 1024], P('seq', ('tr', 'tc'))
Inputs may be any that keep to these rules, and one draw needn't show every extreme that they name: `seg_start`: 1 where a segment begins a prompt, 0 where it continues the prompt of the segment before; segment 0 begins a prompt; a prompt spans at most 32 segments, and in every draw one prompt spans exactly that many. `seg_len`: live tokens at the head of each segment; every segment of a prompt but its last is full. `memory_rates`: all three tables lie strictly between 0 and 1.
All inputs are finite; a program needn't handle non-finite values.
Results may differ from a plain program's by a relative error of at most 0.015.
Values may be sent and summed in bfloat16 or wider, within the bound.
No kernel may reach another device: no remote copies, remote signals or barrier semaphores. Data moves between devices by JAX's collectives and lax.ppermute only.
A program may use at most 192 MiB of HBM per device.

v0:
```python
import jax
import jax.numpy as jnp
from jax import lax
from jax.sharding import PartitionSpec as P

HD = 128
SEG = 1024
CONV = 4


epsilon = 1e-06
score_scale = 8.0


def passed_along(block, axis, distance):
    devices = range(lax.axis_size(axis))
    route = [(i - distance, i) for i in devices if i - distance in devices]
    return lax.ppermute(block, axis, route)


def carried_in(array, axis, combine, identity):
    count, index = (lax.axis_size(axis), lax.axis_index(axis))
    everything = jax.tree.map(
        lambda part, kind: lax.all_gather(part.astype(kind), axis),
        array,
        (jnp.bfloat16, jnp.bfloat16),
    )
    start = jax.tree.map(
        lambda part, zero: jnp.broadcast_to(jnp.asarray(zero, part.dtype), part.shape),
        array,
        identity,
    )

    def step(k, before):
        reached = k < index
        new = combine(
            before, jax.tree.map(lambda part, own: part[k].astype(own.dtype), everything, array)
        )
        return jax.tree.map(lambda a, b: jnp.where(reached, a, b), new, before)

    return lax.fori_loop(0, count, step, start)


def unit_rows(values_in):
    return values_in * lax.rsqrt(jnp.sum(values_in * values_in, -1, keepdims=True) + epsilon)


def exact_product(left, right):
    return jnp.matmul(left, right, precision=lax.Precision.HIGHEST)


def combine(earlier, later):
    return (exact_product(later[0], earlier[0]), exact_product(later[0], earlier[1]) + later[1])


def body(
    activations,
    seg_len,
    seg_start,
    memory_rates,
    w_qkv,
    conv_w,
    persistent,
    w_out,
    w_gate,
    w_up,
    w_down,
):
    token_rows, local_feat = activations.shape
    seg_count = seg_len.shape[0]
    full_width = w_qkv.shape[0]
    head_width = w_qkv.shape[2]
    local_heads = head_width // HD
    group_index = lax.axis_index(("tr", "tc"))
    wide = w_qkv.reshape(full_width, 3 * head_width)
    row_ids = jnp.arange(token_rows, dtype=jnp.int32)
    position = row_ids % SEG
    segment_of = row_ids // SEG
    continuing = seg_start[segment_of] == 0
    piece = lax.all_gather(activations, ("tr", "tc"), axis=1, tiled=True)
    piece_f = piece.astype(jnp.float32)
    projected = jnp.dot(piece, wide, preferred_element_type=jnp.float32)
    squares = jnp.sum(piece_f * piece_f, -1)
    qkv = (projected * lax.rsqrt(squares / full_width + epsilon)[:, None]).astype(jnp.bfloat16)
    edge_rows = passed_along(qkv[token_rows - (CONV - 1) :], "seq", 1)
    extended = jnp.concatenate([edge_rows, qkv], 0)
    taps = conv_w.reshape(CONV, 3 * head_width)
    convolved = jnp.zeros((token_rows, 3 * head_width), jnp.float32)
    for offset in range(CONV):
        shifted = extended[CONV - 1 - offset : CONV - 1 - offset + token_rows].astype(jnp.float32)
        valid = (position >= offset) | continuing
        convolved = convolved + jnp.where(valid[:, None], taps[offset] * shifted, 0.0)
    parts = convolved.reshape(token_rows, 3, local_heads, HD)
    query_n = unit_rows(parts[:, 0]).astype(jnp.bfloat16)
    key_n = unit_rows(parts[:, 1]).astype(jnp.bfloat16)
    value_n = parts[:, 2].astype(jnp.bfloat16)
    pkeys = unit_rows(persistent[0].astype(jnp.float32).reshape(-1, local_heads, HD)).astype(
        jnp.bfloat16
    )
    pvalues = persistent[1].reshape(-1, local_heads, HD)
    persist_rows = pkeys.shape[0]
    live = position < seg_len[segment_of]
    keys_live = jnp.where(live[:, None, None], key_n, jnp.zeros((), jnp.bfloat16)).reshape(
        seg_count, SEG, local_heads, HD
    )
    value_segs = value_n.reshape(seg_count, SEG, local_heads, HD)
    a_mats = jnp.einsum("cthi,cthj->chij", keys_live, keys_live, preferred_element_type=jnp.float32)
    b_mats = jnp.einsum(
        "cthi,cthj->chij", keys_live, value_segs, preferred_element_type=jnp.float32
    )
    my_rates = lax.dynamic_slice_in_dim(memory_rates, group_index * local_heads, local_heads, 2)
    decay_factor = my_rates[0][:, :, None, None]
    eta = my_rates[1][:, :, None, None]
    theta = my_rates[2][:, :, None, None]
    keep = (1 - seg_start).astype(jnp.float32)[:, None, None, None]
    identity = jnp.eye(HD, dtype=jnp.float32)
    upper = jnp.concatenate([(1.0 - decay_factor) * identity - theta * a_mats, eta * identity], -1)
    lower = jnp.concatenate([-theta * a_mats, eta * identity], -1)
    seg_maps = jnp.concatenate([upper, lower], -2) * keep
    seg_shifts = jnp.concatenate([theta * b_mats, theta * b_mats], -2)
    dev_map = seg_maps[0]
    dev_shift = seg_shifts[0]
    neutral = (
        jnp.broadcast_to(jnp.eye(2 * HD, dtype=jnp.float32), dev_map.shape),
        jnp.zeros_like(dev_shift),
    )
    _, state = carried_in((dev_map, dev_shift), "seq", combine, neutral)
    seg_index = 0
    memory_in = state[:, :HD] * keep[seg_index]
    query_seg = query_n.astype(jnp.float32)
    retr_parts = jnp.einsum("thi,hij->thj", query_seg, memory_in, precision=lax.Precision.HIGHEST)
    mem = retr_parts * lax.rsqrt(jnp.mean(retr_parts * retr_parts, -1, keepdims=True) + epsilon)
    block_rows = min(512, SEG)
    attn_parts = []
    seg_index = 0
    first = seg_index * SEG
    keys_all = jnp.concatenate([pkeys, key_n], 0)
    values_all = jnp.concatenate([pvalues, value_n], 0)
    cols_k = jnp.arange(persist_rows + SEG, dtype=jnp.int32)[None, :] - persist_rows
    for block_start in range(0, SEG, block_rows):
        query_blk = query_n[first + block_start : first + block_start + block_rows]
        scores = score_scale * jnp.einsum(
            "qhd,khd->hqk", query_blk, keys_all, preferred_element_type=jnp.float32
        )
        rows_q = block_start + jnp.arange(block_rows, dtype=jnp.int32)[:, None]
        allow = (cols_k < 0) | (cols_k <= rows_q) & (cols_k < seg_len[seg_index])
        weights = jnp.where(allow[None], jnp.exp(scores), 0.0)
        probs = (weights / jnp.sum(weights, -1, keepdims=True)).astype(jnp.bfloat16)
        attn_parts.append(
            jnp.einsum("hqk,khd->qhd", probs, values_all, preferred_element_type=jnp.float32)
        )
    attn = jnp.concatenate(attn_parts, 0)
    heads_out = (attn + mem).astype(jnp.bfloat16).reshape(token_rows, head_width)
    partial_value = jnp.dot(heads_out, w_out, preferred_element_type=jnp.float32)
    share = lax.psum_scatter(
        partial_value.astype(jnp.bfloat16), ("tr", "tc"), scatter_dimension=1, tiled=True
    ).astype(jnp.float32)
    resid = (activations.astype(jnp.float32) + share).astype(jnp.bfloat16)
    piece = lax.all_gather(resid, ("tr", "tc"), axis=1, tiled=True)
    piece_f = piece.astype(jnp.float32)
    gate = jnp.dot(piece, w_gate, preferred_element_type=jnp.float32)
    up_proj = jnp.dot(piece, w_up, preferred_element_type=jnp.float32)
    squares2 = jnp.sum(piece_f * piece_f, -1)
    inv_rms2 = lax.rsqrt(squares2 / full_width + epsilon)[:, None]
    hidden = (jax.nn.silu(gate * inv_rms2) * (up_proj * inv_rms2)).astype(jnp.bfloat16)
    down = jnp.dot(hidden, w_down, preferred_element_type=jnp.float32)
    ffn_share = lax.psum_scatter(
        down.astype(jnp.bfloat16), ("tr", "tc"), scatter_dimension=1, tiled=True
    ).astype(jnp.float32)
    return (resid.astype(jnp.float32) + ffn_share).astype(jnp.bfloat16)


def solution(mesh):
    return jax.shard_map(
        body,
        mesh=mesh,
        in_specs=(
            P("seq", ("tr", "tc")),
            P("seq"),
            P("seq"),
            P(None, "seq", None),
            P(None, None, ("tr", "tc")),
            P(None, None, ("tr", "tc")),
            P(None, None, ("tr", "tc")),
            P(("tr", "tc"), None),
            P(None, ("tr", "tc")),
            P(None, ("tr", "tc")),
            P(("tr", "tc"), None),
        ),
        out_specs=P("seq", ("tr", "tc")),
        check_vma=False,
    )
```

profile of v0, /device:TPU:14, one launch (start us, length us, event | category | flops | bytes accessed | tf_op | source)
XLA Modules:
  0.0 543.9 jit_solution(447343479801649792)
XLA Ops:
  8.0 2.6 copy.46
  11.4 51.8 %all-gather.5.cloned.1.call-done = bf16[1024,1024]{1,0:T(8,128)(2,1)} async-done(((bf16[1024,256]{1,0:T(8,128)(2,1)}), bf16[1024,1024]{1,0:T(8,128)(2,1)}) %all-gather.5.cloned.1.call-update) | async-done | bytes 2097168 | tf_op jit(solution)/shard_map/all_gather | solution.py:80
  63.1 2.1 multiply_reduce_fusion.1
  65.2 3.9 multiply_convert_fusion
  69.1 1.9 collective-permute-start
  71.2 5.0 collective-permute-done
  76.2 3.8 select_add_fusion
  80.0 5.2 reshape.355
  85.2 1.7 fusion.62
  86.9 1.6 slice.86
  93.8 2.2 fusion.15
  96.7 3.0 fusion.11
  99.7 5.4 fusion.20
  105.1 4.0 fusion.9
  109.1 5.3 fusion.21
  114.4 59.0 %all-gather.9.cloned.1.call-done = bf16[64,2,256,128]{3,2,1,0:T(8,128)(2,1)} async-done(((bf16[1,2,256,128]{3,2,1,0:T(8,128)(2,1)}), bf16[64,2,256,128]{3,2,1,0:T(8,128)(2,1)}) %all-gather.9.cloned.1.call-update) | async-done | bytes 8388624 | tf_op jit(solution)/shard_map/all_gather | solution.py:24
  173.4 98.8 %all-gather.7.cloned.1.call-done = bf16[64,2,256,256]{3,2,1,0:T(8,128)(2,1)} async-done(((bf16[1,2,256,256]{3,2,1,0:T(8,128)(2,1)}), bf16[64,2,256,256]{3,2,1,0:T(8,128)(2,1)}) %all-gather.7.cloned.1.call-update) | async-done | bytes 16777232 | tf_op jit(solution)/shard_map/all_gather | solution.py:24
  272.3 92.7 %while.14 = (s32[]{:T(128)}, f32[2,256,128]{2,1,0:T(8,128)S(1)}, s32[]{:T(128)}, bf16[64,2,256,256]{3,2,1,0:T(8,128)(2,1)}, bf16[64,2,256,128]{3,2,1,0:T(8,128)(2,1)}, /*index=5*/s32[]{:T(128)}, s32[]{:T(128)}) while((s32[]{:T(128)}, f32[2,256,128]{2,1,0:T(8,128)S(1)}, s32[]{:T(128)}, bf16[64,2,256,256]{3,2,1,0:T(8,128)(2,1)}, ...), condition=%wide.region_7.8_spmd.clone, body=%wide.region_6.7_spmd.clone.sunk | while | flops 201654272 | bytes 1706599 | solution.py:41
  272.3 1.4 fusion.83
  282.4 1.4 fusion.83
  283.9 1.4 fusion.83
  285.3 1.4 fusion.83
  286.8 1.4 fusion.83
  367.0 3.2 convolution_convert_fusion
  370.3 46.4 %reduce-scatter.3.cloned.1.call-done = bf16[1024,256]{1,0:T(8,128)(2,1)} async-done(((bf16[1024,1024]{1,0:T(8,128)(2,1)}), bf16[1024,256]{1,0:T(8,128)(2,1)}) %reduce-scatter.3.cloned.1.call-update) | async-done | bytes 524304 | tf_op jit(solution)/shard_map/reduce_scatter | solution.py:155
  416.7 2.0 add_convert_fusion.1
  419.0 52.1 %all-gather.11.cloned.1.call-done = bf16[1024,1024]{1,0:T(8,128)(2,1)} async-done(((bf16[1024,256]{1,0:T(8,128)(2,1)}), bf16[1024,1024]{1,0:T(8,128)(2,1)}) %all-gather.11.cloned.1.call-update) | async-done | bytes 2097168 | tf_op jit(solution)/shard_map/all_gather | solution.py:159
  471.1 2.1 multiply_reduce_fusion
  473.1 4.9 fusion.64
  478.1 7.8 %convolution_convert_fusion.1 = bf16[1024,1024]{1,0:T(8,128)(2,1)} fusion(bf16[704,1024]{1,0:T(8,128)(2,1)S(1)} %copy-done, f32[1024,704]{0,1:T(8,128)} %fusion.64, bf16[1024,1024]{1,0:T(8,128)(2,1)} %all-gather.11.cloned.1.call-done, bf16[1024,704]{0,1:T(8,128)(2,1)} %param.22, f32[1024]{0:T(1024)S(1)} %add_rsqrt_fusion.3), kind=kOutput, calls=%fused_computation.31 | convolution fusion | flops 2959605760 | bytes 9965568 | tf_op jit(solution)/shard_map/dot_general | solution.py:166
  485.9 49.2 %reduce-scatter.5.cloned.1.call-done = bf16[1024,256]{1,0:T(8,128)(2,1)} async-done(((bf16[1024,1024]{1,0:T(8,128)(2,1)}), bf16[1024,256]{1,0:T(8,128)(2,1)}) %reduce-scatter.5.cloned.1.call-update) | async-done | bytes 524304 | tf_op jit(solution)/shard_map/reduce_scatter | solution.py:167
  535.1 2.0 add_convert_fusion
  (203 shorter events, 92.4 us)
Async XLA Ops:
  6.5 471.5 %copy-start = (bf16[704,1024]{1,0:T(8,128)(2,1)S(1)}, bf16[704,1024]{1,0:T(8,128)(2,1)}, u32[]{:S(2)}) copy-start(bf16[704,1024]{1,0:T(8,128)(2,1)} %param.23) | copy-start | bytes 4325380
  6.5 4.8 copy-start.9
  6.5 56.6 %all-gather.5.cloned.1.call-start = ((), (), s32[]{:S(2)}) async-start(), calls=%async_computation.2 | async-start | bytes 2621440 | tf_op jit(solution)/shard_map/all_gather | solution.py:80
  7.3 166.2 %all-gather.9.cloned.1.call-start = ((), (), s32[]{:S(2)}) async-start(), calls=%async_computation.4 | async-start | bytes 8519680 | tf_op jit(solution)/shard_map/all_gather | solution.py:24
  65.2 5.8 %copy-start.10 = (f32[3,1,8]{2,1,0:T(1,128)S(1)}, f32[3,1,8]{2,1,0:T(1,128)}, u32[]{:S(2)}) copy-start(f32[3,1,8]{2,1,0:T(1,128)} %param.16) | copy-start | bytes 292
  69.1 7.1 %collective-permute-start = (bf16[3,768]{1,0:T(4,128)(2,1)S(1)}, bf16[3,768]{1,0:T(4,128)(2,1)S(1)}, u32[]{:S(2)}, u32[]{:S(2)}) collective-permute-start(bf16[3,768]{1,0:T(4,128)(2,1)S(1)} %slice.81), channel_id=1, source_target_pairs={{0,4},{4,8},{8,12},{12,16},{16,20},{20,24},{24,28},{28,32},{32,36}... | collective-permute-start | bytes 13832 | tf_op jit(solution)/shard_map/ppermute | solution.py:18
  89.2 3.1 copy-start.4
  89.2 4.3 copy-start.8
  89.3 0.9 copy-start.7
  91.4 180.8 %all-gather.7.cloned.1.call-start = ((), (), s32[]{:S(2)}) async-start(), calls=%async_computation.3 | async-start | bytes 17039360 | tf_op jit(solution)/shard_map/all_gather | solution.py:24
  93.2 323.5 %reduce-scatter.3.cloned.1.call-start = ((), (), s32[]{:S(2)}) async-start(), calls=%async_computation.5 | async-start | bytes 2621440 | tf_op jit(solution)/shard_map/reduce_scatter | solution.py:155
  93.7 3.0 copy-start.5
  99.7 5.4 copy-start.3
  272.3 93.5 %copy-start.6 = (f32[512,2,128]{0,2,1:T(8,128)S(1)}, f32[512,2,128]{0,2,1:T(8,128)}, u32[]{:S(2)}) copy-start(f32[512,2,128]{0,2,1:T(8,128)} %fusion.20) | copy-start | bytes 1572868
  367.0 49.7 %copy-start.2 = (bf16[1024,256]{1,0:T(8,128)(2,1)S(1)}, bf16[1024,256]{1,0:T(8,128)(2,1)}, u32[]{:S(2)}) copy-start(bf16[1024,256]{1,0:T(8,128)(2,1)} %param.13) | copy-start | bytes 1572868
  370.2 102.9 %copy-start.11 = (bf16[1024,704]{0,1:T(8,128)(2,1)S(1)}, bf16[1024,704]{0,1:T(8,128)(2,1)}, u32[]{:S(2)}) copy-start(bf16[1024,704]{0,1:T(8,128)(2,1)} %param.21) | copy-start | bytes 4325380
  370.3 100.8 %all-gather.11.cloned.1.call-start = ((), (), s32[]{:S(2)}) async-start(), calls=%async_computation.6 | async-start | bytes 2621440 | tf_op jit(solution)/shard_map/all_gather | solution.py:159
  418.7 116.4 %reduce-scatter.5.cloned.1.call-start = ((), (), s32[]{:S(2)}) async-start(), calls=%async_computation.7 | async-start | bytes 2621440 | tf_op jit(solution)/shard_map/reduce_scatter | solution.py:167
  478.1 57.0 %copy-start.1 = (bf16[1024,256]{1,0:T(8,128)(2,1)S(1)}, bf16[1024,256]{1,0:T(8,128)(2,1)}, u32[]{:S(2)}) copy-start(bf16[1024,256]{1,0:T(8,128)(2,1)} %add_convert_fusion.1) | copy-start | bytes 1572868
Sparse Core Ops, SparseCore 0:
  9.1 53.9 all-gather.4
  91.6 81.8 all-gather.8
  176.2 96.0 all-gather.6
  370.4 46.3 reduce-scatter.2
  418.8 52.1 all-gather.10
  486.0 49.0 reduce-scatter.4
where the time goes:
time: 548 us; the launch traced here: 544 us
  waiting for transfers between devices  363 us (66%)
  matrix products  128 us (23%)
  other arithmetic  17.2 us (3%)
  local copies, waits for them, and re-layouts  15.2 us (3%)
  between operations  15.1 us (3%)
    all_gather x2, waiting for transfers between devices, carried_in(): lax.all_gather(part.astype(kind), axis)  158 us
    dot_general x64, matrix products, exact_product(): return jnp.matmul(left, right, precision=lax.Precision.HIGHEST)  89 us
    all_gather x1, waiting for transfers between devices, body(): piece = lax.all_gather(resid, ('tr', 'tc'), axis=1, tiled=True)  52.1 us
    all_gather x1, waiting for transfers between devices, body(): piece = lax.all_gather(activations, ('tr', 'tc'), axis=1, tiled=True)  51.8 us
    reduce_scatter x1, waiting for transfers between devices, body(): lax.psum_scatter(down.astype(jnp.bfloat16), ('tr', 'tc'), scatter_dimensi...  49.2 us
    reduce_scatter x1, waiting for transfers between devices, body(): lax.psum_scatter(partial_value.astype(jnp.bfloat16), ('tr', 'tc'), scatte...  46.4 us
  transfers between devices with their start and end apart: 7, of which 7 were waited for; matrix products, arithmetic and copies ran while one was open for 5% of the time, Pallas kernels for 0%

commit v1 on v0

--- a/solution.py
+++ b/solution.py
@@ -6,6 +6,7 @@
 HD = 128
 SEG = 1024
 CONV = 4
+PROMPT_SPAN = 32
 
 
 epsilon = 1e-06
@@ -18,27 +19,30 @@
     return lax.ppermute(block, axis, route)
 
 
-def carried_in(array, axis, combine, identity):
-    count, index = (lax.axis_size(axis), lax.axis_index(axis))
-    everything = jax.tree.map(
-        lambda part, kind: lax.all_gather(part.astype(kind), axis),
-        array,
-        (jnp.bfloat16, jnp.bfloat16),
-    )
-    start = jax.tree.map(
-        lambda part, zero: jnp.broadcast_to(jnp.asarray(zero, part.dtype), part.shape),
-        array,
-        identity,
-    )
+def passed_exact(block, axis, distance):
+    high = block.astype(jnp.bfloat16)
+    low = (block - high.astype(jnp.float32)).astype(jnp.bfloat16)
+    high, low = passed_along((high, low), axis, distance)
+    return high.astype(jnp.float32) + low.astype(jnp.float32)
 
-    def step(k, before):
-        reached = k < index
-        new = combine(
-            before, jax.tree.map(lambda part, own: part[k].astype(own.dtype), everything, array)
-        )
-        return jax.tree.map(lambda a, b: jnp.where(reached, a, b), new, before)
 
-    return lax.fori_loop(0, count, step, start)
+def window_scan(seg_map, seg_shift, axis, reach):
+    distance = 1
+    while distance < reach:
+        if 2 * distance >= reach:
+            shift_before = passed_exact(seg_shift, axis, distance)
+            seg_shift = exact_product(seg_map, shift_before) + seg_shift
+        else:
+            high = seg_shift.astype(jnp.bfloat16)
+            low = (seg_shift - high.astype(jnp.float32)).astype(jnp.bfloat16)
+            map_before, high, low = passed_along(
+                (seg_map.astype(jnp.bfloat16), high, low), axis, distance
+            )
+            shift_before = high.astype(jnp.float32) + low.astype(jnp.float32)
+            seg_shift = exact_product(seg_map, shift_before) + seg_shift
+            seg_map = exact_product(seg_map, map_before.astype(jnp.float32))
+        distance *= 2
+    return seg_shift
 
 
 def unit_rows(values_in):
@@ -47,10 +51,6 @@
 
 def exact_product(left, right):
     return jnp.matmul(left, right, precision=lax.Precision.HIGHEST)
-
-
-def combine(earlier, later):
-    return (exact_product(later[0], earlier[0]), exact_product(later[0], earlier[1]) + later[1])
 
 
 def body(
@@ -118,15 +118,9 @@
     lower = jnp.concatenate([-theta * a_mats, eta * identity], -1)
     seg_maps = jnp.concatenate([upper, lower], -2) * keep
     seg_shifts = jnp.concatenate([theta * b_mats, theta * b_mats], -2)
-    dev_map = seg_maps[0]
-    dev_shift = seg_shifts[0]
-    neutral = (
-        jnp.broadcast_to(jnp.eye(2 * HD, dtype=jnp.float32), dev_map.shape),
-        jnp.zeros_like(dev_shift),
-    )
-    _, state = carried_in((dev_map, dev_shift), "seq", combine, neutral)
-    seg_index = 0
-    memory_in = state[:, :HD] * keep[seg_index]
+    reach = min(PROMPT_SPAN, lax.axis_size("seq"))
+    state_out = window_scan(seg_maps[0], seg_shifts[0], "seq", reach)
+    memory_in = passed_exact(state_out[:, :HD], "seq", 1) * keep[0]
     query_seg = query_n.astype(jnp.float32)
     retr_parts = jnp.einsum("thi,hij->thj", query_seg, memory_in, precision=lax.Precision.HIGHEST)
     mem = retr_parts * lax.rsqrt(jnp.mean(retr_parts * retr_parts, -1, keepdims=True) + epsilon)

time: 548 us -> 372 us (0.68)
  waiting for transfers between devices: 363 us -> 223 us
  matrix products: 128 us -> 41.5 us
  starting transfers between devices: 2.53 us -> 57.8 us
    all_gather x2 -> x0, waiting for transfers between devices: 158 us -> none  [carried_in(): lax.all_gather(part.astype(kind), axis)]
    dot_general x64 -> x9, matrix products: 89 us -> 6.05 us  [exact_product(): return jnp.matmul(left, right, precision=lax.Precision.HIGHEST)]
    ppermute x1 -> x17, starting transfers between devices: 1.92 us -> 57.5 us  [passed_along(): return lax.ppermute(block, axis, route)]
    ppermute x1 -> x17, waiting for transfers between devices: 5.01 us -> 28.3 us  [passed_along(): return lax.ppermute(block, axis, route)]
  transfers between devices with their start and end apart: 7 -> 21, of which waited for: 7 -> 12; matrix products, arithmetic and copies ran while one was open for 5% -> 8% of each run, Pallas kernels for 0% -> 0%
where the time goes in v1:
time: 372 us; the launch traced here: 369 us
  waiting for transfers between devices  223 us (60%)
  starting transfers between devices  57.8 us (16%)
  matrix products  41.5 us (11%)
  other arithmetic  20.5 us (6%)
  between operations  15.1 us (4%)
  local copies, waits for them, and re-layouts  11.4 us (3%)
    ppermute x17, starting transfers between devices, passed_along(): return lax.ppermute(block, axis, route)  57.5 us
    all_gather x1, waiting for transfers between devices, body(): piece = lax.all_gather(resid, ('tr', 'tc'), axis=1, tiled=True)  52.1 us
    reduce_scatter x1, waiting for transfers between devices, body(): lax.psum_scatter(down.astype(jnp.bfloat16), ('tr', 'tc'), scatter_dimensi...  49.2 us
    all_gather x1, waiting for transfers between devices, body(): piece = lax.all_gather(activations, ('tr', 'tc'), axis=1, tiled=True)  46.8 us
    reduce_scatter x1, waiting for transfers between devices, body(): lax.psum_scatter(partial_value.astype(jnp.bfloat16), ('tr', 'tc'), scatte...  45.5 us
    ppermute x17, waiting for transfers between devices, passed_along(): return lax.ppermute(block, axis, route)  28.3 us
    dot_general x2, matrix products, body(): jnp.einsum('hqk,khd->qhd', probs, values_all, preferred_element_type=jnp....  9.03 us
    dot_general x1, matrix products, body(): down = jnp.dot(hidden, w_down, preferred_element_type=jnp.float32)  7.81 us
  transfers between devices with their start and end apart: 21, of which 12 were waited for; matrix products, arithmetic and copies ran while one was open for 8% of the time, Pallas kernels for 0%

profile of v1, /device:TPU:14, one launch (start us, length us, event | category | flops | bytes accessed | tf_op | source)
XLA Modules:
  0.0 369.0 jit_solution(2655117677076065765)
XLA Ops:
  9.5 2.6 copy.76
  16.3 46.8 %all-gather.3.cloned.1.call-done = bf16[1024,1024]{1,0:T(8,128)(2,1)} async-done(((bf16[1024,256]{1,0:T(8,128)(2,1)}), bf16[1024,1024]{1,0:T(8,128)(2,1)}) %all-gather.3.cloned.1.call-update) | async-done | bytes 2097168 | tf_op jit(solution)/shard_map/all_gather | solution.py:80
  63.1 2.1 multiply_reduce_fusion.1
  65.2 3.9 %multiply_convert_fusion = bf16[1024,768]{1,0:T(8,128)(2,1)S(1)} fusion(bf16[1024,1024]{1,0:T(8,128)(2,1)} %all-gather.3.cloned.1.call-done, bf16[1024,768]{0,1:T(8,128)(2,1)} %bitcast.82, f32[1024]{0:T(1024)S(1)} %add_rsqrt_fusion.4), kind=kOutput, calls=%fused_computation.11 | convolution fusion | flops 1612185600 | bytes 5246976 | tf_op jit(solution)/shard_map/dot_general | solution.py:82
  71.7 4.5 %collective-permute-done = bf16[3,768]{1,0:T(4,128)(2,1)S(1)} collective-permute-done((bf16[3,768]{1,0:T(4,128)(2,1)S(1)}, bf16[3,768]{1,0:T(4,128)(2,1)S(1)}, u32[]{:S(2)}, u32[]{:S(2)}) %collective-permute-start) | collective-permute-done | bytes 4640 | tf_op jit(solution)/shard_map/ppermute | solution.py:19
  76.2 3.8 %select_add_fusion = f32[1024,768]{1,0:T(8,128)} fusion(bf16[1024,768]{1,0:T(8,128)(2,1)S(1)} %multiply_convert_fusion, bf16[3,768]{1,0:T(4,128)(2,1)S(1)} %collective-permute-done, f32[768]{0:T(1024)S(1)} %mul.251, f32[768]{0:T(1024)S(1)} %mul.248, f32[768]{0:T(1024)S(1)} %mul.245, f32[768]{0:T(1024)S(1)} %mul.239, ...), kind=kLoop, calls=%fused_computation.10 | loop fusion | flops 18874368 | bytes 4739584 | tf_op jit(solution)/shard_map/add | solution.py:92
  80.0 5.2 %reshape.298 = f32[1024,3,2,128]{3,2,1,0:T(2,128)} reshape(f32[1024,768]{1,0:T(8,128)} %select_add_fusion) | data formatting | bytes 6291456 | tf_op jit(solution)/shard_map/reshape | solution.py:93
  98.6 3.0 fusion.3
  101.6 3.0 fusion.1
  104.5 4.5 %fusion.12 = f32[512,2,128]{0,2,1:T(8,128)S(1)} fusion(f32[2,512,1040]{1,2,0:T(8,128)} %fusion.3, bf16[1024,2,128]{2,0,1:T(8,128)(2,1)} %bitcast.84, bf16[16,2,128]{2,0,1:T(8,128)(2,1)S(1)} %copy.78), kind=kOutput, calls=%fused_computation.29 | convolution fusion | flops 275826688 | bytes 5316608 | tf_op jit(solution)/shard_map/hqk,khd->qhd/dot_general | solution.py:144
  110.5 3.0 collective-permute-start.8
  113.5 4.2 %collective-permute-start.7 = (bf16[2,256,128]{1,2,0:T(8,128)(2,1)S(1)}, bf16[2,256,128]{1,2,0:T(8,128)(2,1)S(1)}, u32[]{:S(2)}, u32[]{:S(2)}) collective-permute-start(bf16[2,256,128]{1,2,0:T(8,128)(2,1)S(1)} %get-tuple-element.18), channel_id=1, source_target_pairs={{0,8},{4,12},{8,16},{12,20},{16,24},{20,28},{24,32},{28,36},{32,40... | collective-permute-start | bytes 393224 | tf_op jit(solution)/shard_map/ppermute | solution.py:19
  118.4 5.3 %collective-permute-start.2 = (bf16[2,256,256]{2,1,0:T(8,128)(2,1)S(1)}, bf16[2,256,256]{2,1,0:T(8,128)(2,1)S(1)}, u32[]{:S(2)}, u32[]{:S(2)}) collective-permute-start(bf16[2,256,256]{2,1,0:T(8,128)(2,1)S(1)} %get-tuple-element.34), channel_id=1, source_target_pairs={{0,8},{4,12},{8,16},{12,20},{16,24},{20,28},{24,32},{28,36},{32,40... | collective-permute-start | bytes 786440 | tf_op jit(solution)/shard_map/ppermute | solution.py:19
  124.5 4.1 %collective-permute-start.10 = (bf16[2,256,128]{1,2,0:T(8,128)(2,1)S(1)}, bf16[2,256,128]{1,2,0:T(8,128)(2,1)S(1)}, u32[]{:S(2)}, u32[]{:S(2)}) collective-permute-start(bf16[2,256,128]{1,2,0:T(8,128)(2,1)S(1)} %get-tuple-element.15), channel_id=1, source_target_pairs={{0,16},{4,20},{8,24},{12,28},{16,32},{20,36},{24,40},{28,44},{32,4... | collective-permute-start | bytes 393224 | tf_op jit(solution)/shard_map/ppermute | solution.py:19
  128.6 3.6 collective-permute-start.9
  132.6 2.8 collective-permute-start.3
  135.4 5.3 %collective-permute-done.10 = bf16[2,256,128]{1,2,0:T(8,128)(2,1)S(1)} collective-permute-done((bf16[2,256,128]{1,2,0:T(8,128)(2,1)S(1)}, bf16[2,256,128]{1,2,0:T(8,128)(2,1)S(1)}, u32[]{:S(2)}, u32[]{:S(2)}) %collective-permute-start.10) | collective-permute-done | bytes 131104 | tf_op jit(solution)/shard_map/ppermute | solution.py:19
  140.6 8.1 %collective-permute-done.9 = bf16[2,256,128]{1,2,0:T(8,128)(2,1)S(1)} collective-permute-done((bf16[2,256,128]{1,2,0:T(8,128)(2,1)S(1)}, bf16[2,256,128]{1,2,0:T(8,128)(2,1)S(1)}, u32[]{:S(2)}, u32[]{:S(2)}) %collective-permute-start.9) | collective-permute-done | bytes 131104 | tf_op jit(solution)/shard_map/ppermute | solution.py:19
  149.4 3.4 collective-permute-start.12
  152.8 7.5 %collective-permute-start.11 = (bf16[2,256,128]{1,2,0:T(8,128)(2,1)S(1)}, bf16[2,256,128]{1,2,0:T(8,128)(2,1)S(1)}, u32[]{:S(2)}, u32[]{:S(2)}) collective-permute-start(bf16[2,256,128]{1,2,0:T(8,128)(2,1)S(1)} %get-tuple-element.14), channel_id=1, source_target_pairs={{0,32},{4,36},{8,40},{12,44},{16,48},{20,52},{24,56},{28,60},{32,6... | collective-permute-start | bytes 393224 | tf_op jit(solution)/shard_map/ppermute | solution.py:19
  160.7 3.1 collective-permute-start.4
  164.2 4.4 %collective-permute-done.11 = bf16[2,256,128]{1,2,0:T(8,128)(2,1)S(1)} collective-permute-done((bf16[2,256,128]{1,2,0:T(8,128)(2,1)S(1)}, bf16[2,256,128]{1,2,0:T(8,128)(2,1)S(1)}, u32[]{:S(2)}, u32[]{:S(2)}) %collective-permute-start.11) | collective-permute-done | bytes 131104 | tf_op jit(solution)/shard_map/ppermute | solution.py:19
  169.2 7.1 %collective-permute-start.14 = (bf16[2,256,128]{1,2,0:T(8,128)(2,1)S(1)}, bf16[2,256,128]{1,2,0:T(8,128)(2,1)S(1)}, u32[]{:S(2)}, u32[]{:S(2)}) collective-permute-start(bf16[2,256,128]{1,2,0:T(8,128)(2,1)S(1)} %get-tuple-element.11), channel_id=1, source_target_pairs={{0,64},{4,68},{8,72},{12,76},{16,80},{20,84},{24,88},{28,92},{32,9... | collective-permute-start | bytes 393224 | tf_op jit(solution)/shard_map/ppermute | solution.py:19
  178.9 4.4 %collective-permute-done.13 = bf16[2,256,128]{1,2,0:T(8,128)(2,1)S(1)} collective-permute-done((bf16[2,256,128]{1,2,0:T(8,128)(2,1)S(1)}, bf16[2,256,128]{1,2,0:T(8,128)(2,1)S(1)}, u32[]{:S(2)}, u32[]{:S(2)}) %collective-permute-start.13) | collective-permute-done | bytes 131104 | tf_op jit(solution)/shard_map/ppermute | solution.py:19
  187.8 4.5 %fusion.13 = f32[512,2,128]{0,2,1:T(8,128)S(1)} fusion(f32[2,512,1040]{1,2,0:T(8,128)} %fusion.1, bf16[1024,2,128]{2,0,1:T(8,128)(2,1)} %bitcast.85, bf16[16,2,128]{2,0,1:T(8,128)(2,1)S(1)} %copy.78), kind=kOutput, calls=%fused_computation.30 | convolution fusion | flops 275826688 | bytes 5316608 | tf_op jit(solution)/shard_map/hqk,khd->qhd/dot_general | solution.py:144
  194.5 2.1 convolution_convert_fusion
  196.6 45.5 %reduce-scatter.3.cloned.1.call-done = bf16[1024,256]{1,0:T(8,128)(2,1)} async-done(((bf16[1024,1024]{1,0:T(8,128)(2,1)}), bf16[1024,256]{1,0:T(8,128)(2,1)}) %reduce-scatter.3.cloned.1.call-update) | async-done | bytes 524304 | tf_op jit(solution)/shard_map/reduce_scatter | solution.py:149
  244.4 52.1 %all-gather.5.cloned.1.call-done = bf16[1024,1024]{1,0:T(8,128)(2,1)} async-done(((bf16[1024,256]{1,0:T(8,128)(2,1)}), bf16[1024,1024]{1,0:T(8,128)(2,1)}) %all-gather.5.cloned.1.call-update) | async-done | bytes 2097168 | tf_op jit(solution)/shard_map/all_gather | solution.py:153
  296.5 2.1 multiply_reduce_fusion
  298.6 4.9 %fusion.91 = f32[1024,704]{0,1:T(8,128)} fusion(bf16[1024,1024]{1,0:T(8,128)(2,1)} %all-gather.5.cloned.1.call-done, bf16[1024,704]{0,1:T(8,128)(2,1)S(1)} %copy-done.15), kind=kOutput, calls=%fused_computation.159 | convolution fusion | flops 1476395008 | bytes 6422528 | tf_op jit(solution)/shard_map/dot_general | solution.py:155
  303.5 7.8 %convolution_convert_fusion.1 = bf16[1024,1024]{1,0:T(8,128)(2,1)} fusion(bf16[704,1024]{1,0:T(8,128)(2,1)S(1)} %copy-done, f32[1024,704]{0,1:T(8,128)} %fusion.91, bf16[1024,1024]{1,0:T(8,128)(2,1)} %all-gather.5.cloned.1.call-done, bf16[1024,704]{0,1:T(8,128)(2,1)} %param.20, f32[1024]{0:T(1024)S(1)} %add_rsqrt_fusion.3), kind=kOutput, calls=%fused_computation.22 | convolution fusion | flops 2959605760 | bytes 9965568 | tf_op jit(solution)/shard_map/dot_general | solution.py:160
  311.3 49.2 %reduce-scatter.5.cloned.1.call-done = bf16[1024,256]{1,0:T(8,128)(2,1)} async-done(((bf16[1024,1024]{1,0:T(8,128)(2,1)}), bf16[1024,256]{1,0:T(8,128)(2,1)}) %reduce-scatter.5.cloned.1.call-update) | async-done | bytes 524304 | tf_op jit(solution)/shard_map/reduce_scatter | solution.py:161
  (118 shorter events, 40.2 us)
Async XLA Ops:
  6.5 296.9 %copy-start = (bf16[704,1024]{1,0:T(8,128)(2,1)S(1)}, bf16[704,1024]{1,0:T(8,128)(2,1)}, u32[]{:S(2)}) copy-start(bf16[704,1024]{1,0:T(8,128)(2,1)} %param.21) | copy-start | bytes 4325380
  6.5 6.9 %copy-start.10 = (f32[4,3,256]{2,0,1:T(4,128)S(1)}, f32[4,3,256]{2,0,1:T(4,128)}, u32[]{:S(2)}) copy-start(f32[4,3,256]{2,0,1:T(4,128)} %param.16) | copy-start | bytes 36868
  6.5 56.6 %all-gather.3.cloned.1.call-start = ((), (), s32[]{:S(2)}) async-start(), calls=%async_computation.2 | async-start | bytes 2621440 | tf_op jit(solution)/shard_map/all_gather | solution.py:80
  7.3 234.9 %reduce-scatter.3.cloned.1.call-start = ((), (), s32[]{:S(2)}) async-start(), calls=%async_computation.3 | async-start | bytes 2621440 | tf_op jit(solution)/shard_map/reduce_scatter | solution.py:149
  13.5 55.6 %copy-start.8 = (f32[128,128]{0,1:T(8,128)}, f32[128,128]{0,1:T(8,128)S(1)}, u32[]{:S(2)}) copy-start(f32[128,128]{0,1:T(8,128)S(1)} %fusion.50) | copy-start | bytes 196612
  69.1 7.1 %collective-permute-start = (bf16[3,768]{1,0:T(4,128)(2,1)S(1)}, bf16[3,768]{1,0:T(4,128)(2,1)S(1)}, u32[]{:S(2)}, u32[]{:S(2)}) collective-permute-start(bf16[3,768]{1,0:T(4,128)(2,1)S(1)} %slice.81), channel_id=1, source_target_pairs={{0,4},{4,8},{8,12},{12,16},{16,20},{20,24},{24,28},{28,32},{32,36}... | collective-permute-start | bytes 13832 | tf_op jit(solution)/shard_map/ppermute | solution.py:19
  89.0 6.2 %copy-start.9 = (f32[128,128]{0,1:T(8,128)S(1)}, f32[128,128]{0,1:T(8,128)}, u32[]{:S(2)}) copy-start(f32[128,128]{0,1:T(8,128)} %copy-done.8) | copy-start | bytes 196612
  89.0 6.2 %copy-start.12 = (f32[2]{0:T(128)S(1)}, f32[2]{0:T(128)}, u32[]{:S(2)}) copy-start(f32[2]{0:T(128)} %get-tuple-element.19) | copy-start | bytes 28
  89.0 6.2 %copy-start.14 = (f32[2]{0:T(128)S(1)}, f32[2]{0:T(128)}, u32[]{:S(2)}) copy-start(f32[2]{0:T(128)} %get-tuple-element.31) | copy-start | bytes 28
  89.4 6.5 %copy-start.5 = (f32[1,2,128,128]{2,3,1,0:T(8,128)S(1)}, f32[1,2,128,128]{2,3,1,0:T(8,128)}, u32[]{:S(2)}) copy-start(f32[1,2,128,128]{2,3,1,0:T(8,128)} %broadcast_multiply_fusion) | copy-start | bytes 393220
  90.6 8.0 %copy-start.4 = (pred[512,1040]{0,1:T(8,128)(4,1)S(1)}, pred[512,1040]{0,1:T(8,128)(4,1)}, u32[]{:S(2)}) copy-start(pred[512,1040]{0,1:T(8,128)(4,1)} %get-tuple-element.30) | copy-start | bytes 1597444
  91.3 17.8 %collective-permute-start.5 = (bf16[2,256,128]{1,2,0:T(8,128)(2,1)}, bf16[2,256,128]{1,2,0:T(8,128)(2,1)}, u32[]{:S(2)}, u32[]{:S(2)}) collective-permute-start(bf16[2,256,128]{1,2,0:T(8,128)(2,1)} %fusion.24), channel_id=1, source_target_pairs={{0,4},{4,8},{8,12},{12,16},{16,20},{20,24},{24,28},{28,32},{32,36}... | collective-permute-start | bytes 393224 | tf_op jit(solution)/shard_map/ppermute | solution.py:19
  93.2 15.8 %collective-permute-start.6 = (bf16[2,256,128]{1,2,0:T(8,128)(2,1)S(1)}, bf16[2,256,128]{1,2,0:T(8,128)(2,1)}, u32[]{:S(2)}, u32[]{:S(2)}) collective-permute-start(bf16[2,256,128]{1,2,0:T(8,128)(2,1)S(1)} %fusion.25), channel_id=1, source_target_pairs={{0,4},{4,8},{8,12},{12,16},{16,20},{20,24},{24,28},{28,32},{32,36}... | collective-permute-start | bytes 393224 | tf_op jit(solution)/shard_map/ppermute | solution.py:19
  96.6 21.2 %collective-permute-start.1 = (bf16[2,256,256]{1,2,0:T(8,128)(2,1)}, bf16[2,256,256]{1,2,0:T(8,128)(2,1)S(1)}, u32[]{:S(2)}, u32[]{:S(2)}) collective-permute-start(bf16[2,256,256]{1,2,0:T(8,128)(2,1)} %fusion.18), channel_id=1, source_target_pairs={{0,4},{4,8},{8,12},{12,16},{16,20},{20,24},{24,28},{28,32},{32,36}... | collective-permute-start | bytes 786440 | tf_op jit(solution)/shard_map/ppermute | solution.py:19
  110.5 13.2 %collective-permute-start.8 = (bf16[2,256,128]{1,2,0:T(8,128)(2,1)S(1)}, bf16[2,256,128]{1,2,0:T(8,128)(2,1)S(1)}, u32[]{:S(2)}, u32[]{:S(2)}) collective-permute-start(bf16[2,256,128]{1,2,0:T(8,128)(2,1)S(1)} %get-tuple-element.17), channel_id=1, source_target_pairs={{0,8},{4,12},{8,16},{12,20},{16,24},{20,28},{24,32},{28,36},{32,40... | collective-permute-start | bytes 393224 | tf_op jit(solution)/shard_map/ppermute | solution.py:19
  113.5 10.2 %collective-permute-start.7 = (bf16[2,256,128]{1,2,0:T(8,128)(2,1)S(1)}, bf16[2,256,128]{1,2,0:T(8,128)(2,1)S(1)}, u32[]{:S(2)}, u32[]{:S(2)}) collective-permute-start(bf16[2,256,128]{1,2,0:T(8,128)(2,1)S(1)} %get-tuple-element.18), channel_id=1, source_target_pairs={{0,8},{4,12},{8,16},{12,20},{16,24},{20,28},{24,32},{28,36},{32,40... | collective-permute-start | bytes 393224 | tf_op jit(solution)/shard_map/ppermute | solution.py:19
  118.4 13.8 %collective-permute-start.2 = (bf16[2,256,256]{2,1,0:T(8,128)(2,1)S(1)}, bf16[2,256,256]{2,1,0:T(8,128)(2,1)S(1)}, u32[]{:S(2)}, u32[]{:S(2)}) collective-permute-start(bf16[2,256,256]{2,1,0:T(8,128)(2,1)S(1)} %get-tuple-element.34), channel_id=1, source_target_pairs={{0,8},{4,12},{8,16},{12,20},{16,24},{20,28},{24,32},{28,36},{32,40... | collective-permute-start | bytes 786440 | tf_op jit(solution)/shard_map/ppermute | solution.py:19
  124.5 16.2 %collective-permute-start.10 = (bf16[2,256,128]{1,2,0:T(8,128)(2,1)S(1)}, bf16[2,256,128]{1,2,0:T(8,128)(2,1)S(1)}, u32[]{:S(2)}, u32[]{:S(2)}) collective-permute-start(bf16[2,256,128]{1,2,0:T(8,128)(2,1)S(1)} %get-tuple-element.15), channel_id=1, source_target_pairs={{0,16},{4,20},{8,24},{12,28},{16,32},{20,36},{24,40},{28,44},{32,4... | collective-permute-start | bytes 393224 | tf_op jit(solution)/shard_map/ppermute | solution.py:19
  128.6 20.2 %collective-permute-start.9 = (bf16[2,256,128]{1,2,0:T(8,128)(2,1)S(1)}, bf16[2,256,128]{1,2,0:T(8,128)(2,1)S(1)}, u32[]{:S(2)}, u32[]{:S(2)}) collective-permute-start(bf16[2,256,128]{1,2,0:T(8,128)(2,1)S(1)} %get-tuple-element.16), channel_id=1, source_target_pairs={{0,16},{4,20},{8,24},{12,28},{16,32},{20,36},{24,40},{28,44},{32,4... | collective-permute-start | bytes 393224 | tf_op jit(solution)/shard_map/ppermute | solution.py:19
  132.6 27.7 %collective-permute-start.3 = (bf16[2,256,256]{2,1,0:T(8,128)(2,1)S(1)}, bf16[2,256,256]{2,1,0:T(8,128)(2,1)S(1)}, u32[]{:S(2)}, u32[]{:S(2)}) collective-permute-start(bf16[2,256,256]{2,1,0:T(8,128)(2,1)S(1)} %get-tuple-element.37), channel_id=1, source_target_pairs={{0,16},{4,20},{8,24},{12,28},{16,32},{20,36},{24,40},{28,44},{32,4... | collective-permute-start | bytes 786440 | tf_op jit(solution)/shard_map/ppermute | solution.py:19
  149.4 14.7 %collective-permute-start.12 = (bf16[2,256,128]{1,2,0:T(8,128)(2,1)S(1)}, bf16[2,256,128]{1,2,0:T(8,128)(2,1)S(1)}, u32[]{:S(2)}, u32[]{:S(2)}) collective-permute-start(bf16[2,256,128]{1,2,0:T(8,128)(2,1)S(1)} %get-tuple-element.13), channel_id=1, source_target_pairs={{0,32},{4,36},{8,40},{12,44},{16,48},{20,52},{24,56},{28,60},{32,6... | collective-permute-start | bytes 393224 | tf_op jit(solution)/shard_map/ppermute | solution.py:19
  152.8 15.7 %collective-permute-start.11 = (bf16[2,256,128]{1,2,0:T(8,128)(2,1)S(1)}, bf16[2,256,128]{1,2,0:T(8,128)(2,1)S(1)}, u32[]{:S(2)}, u32[]{:S(2)}) collective-permute-start(bf16[2,256,128]{1,2,0:T(8,128)(2,1)S(1)} %get-tuple-element.14), channel_id=1, source_target_pairs={{0,32},{4,36},{8,40},{12,44},{16,48},{20,52},{24,56},{28,60},{32,6... | collective-permute-start | bytes 393224 | tf_op jit(solution)/shard_map/ppermute | solution.py:19
  160.7 17.6 %collective-permute-start.4 = (bf16[2,256,256]{2,1,0:T(8,128)(2,1)S(1)}, bf16[2,256,256]{2,1,0:T(8,128)(2,1)S(1)}, u32[]{:S(2)}, u32[]{:S(2)}) collective-permute-start(bf16[2,256,256]{2,1,0:T(8,128)(2,1)S(1)} %get-tuple-element.40), channel_id=1, source_target_pairs={{0,32},{4,36},{8,40},{12,44},{16,48},{20,52},{24,56},{28,60},{32,6... | collective-permute-start | bytes 786440 | tf_op jit(solution)/shard_map/ppermute | solution.py:19
  169.2 9.6 %collective-permute-start.14 = (bf16[2,256,128]{1,2,0:T(8,128)(2,1)S(1)}, bf16[2,256,128]{1,2,0:T(8,128)(2,1)S(1)}, u32[]{:S(2)}, u32[]{:S(2)}) collective-permute-start(bf16[2,256,128]{1,2,0:T(8,128)(2,1)S(1)} %get-tuple-element.11), channel_id=1, source_target_pairs={{0,64},{4,68},{8,72},{12,76},{16,80},{20,84},{24,88},{28,92},{32,9... | collective-permute-start | bytes 393224 | tf_op jit(solution)/shard_map/ppermute | solution.py:19
  176.4 6.9 %collective-permute-start.13 = (bf16[2,256,128]{1,2,0:T(8,128)(2,1)S(1)}, bf16[2,256,128]{1,2,0:T(8,128)(2,1)S(1)}, u32[]{:S(2)}, u32[]{:S(2)}) collective-permute-start(bf16[2,256,128]{1,2,0:T(8,128)(2,1)S(1)} %get-tuple-element.12), channel_id=1, source_target_pairs={{0,64},{4,68},{8,72},{12,76},{16,80},{20,84},{24,88},{28,92},{32,9... | collective-permute-start | bytes 393224 | tf_op jit(solution)/shard_map/ppermute | solution.py:19
  183.9 8.4 %collective-permute-start.16 = (bf16[2,128,128]{1,2,0:T(8,128)(2,1)S(1)}, bf16[2,128,128]{1,2,0:T(8,128)(2,1)S(1)}, u32[]{:S(2)}, u32[]{:S(2)}) collective-permute-start(bf16[2,128,128]{1,2,0:T(8,128)(2,1)S(1)} %get-tuple-element.9), channel_id=1, source_target_pairs={{0,4},{4,8},{8,12},{12,16},{16,20},{20,24},{24,28},{28,32},{32,36}... | collective-permute-start | bytes 196616 | tf_op jit(solution)/shard_map/ppermute | solution.py:19
  185.9 7.7 %collective-permute-start.15 = (bf16[2,128,128]{1,2,0:T(8,128)(2,1)S(1)}, bf16[2,128,128]{1,2,0:T(8,128)(2,1)S(1)}, u32[]{:S(2)}, u32[]{:S(2)}) collective-permute-start(bf16[2,128,128]{1,2,0:T(8,128)(2,1)S(1)} %get-tuple-element.10), channel_id=1, source_target_pairs={{0,4},{4,8},{8,12},{12,16},{16,20},{20,24},{24,28},{28,32},{32,36}... | collective-permute-start | bytes 196616 | tf_op jit(solution)/shard_map/ppermute | solution.py:19
  194.4 47.7 %copy-start.2 = (bf16[1024,256]{1,0:T(8,128)(2,1)S(1)}, bf16[1024,256]{1,0:T(8,128)(2,1)}, u32[]{:S(2)}) copy-start(bf16[1024,256]{1,0:T(8,128)(2,1)} %param.11) | copy-start | bytes 1572868
  196.5 102.0 %copy-start.15 = (bf16[1024,704]{0,1:T(8,128)(2,1)S(1)}, bf16[1024,704]{0,1:T(8,128)(2,1)}, u32[]{:S(2)}) copy-start(bf16[1024,704]{0,1:T(8,128)(2,1)} %param.19) | copy-start | bytes 4325380
  196.6 99.9 %all-gather.5.cloned.1.call-start = ((), (), s32[]{:S(2)}) async-start(), calls=%async_computation.4 | async-start | bytes 2621440 | tf_op jit(solution)/shard_map/all_gather | solution.py:153
  244.1 116.4 %reduce-scatter.5.cloned.1.call-start = ((), (), s32[]{:S(2)}) async-start(), calls=%async_computation.5 | async-start | bytes 2621440 | tf_op jit(solution)/shard_map/reduce_scatter | solution.py:161
  303.5 57.1 %copy-start.1 = (bf16[1024,256]{1,0:T(8,128)(2,1)S(1)}, bf16[1024,256]{1,0:T(8,128)(2,1)}, u32[]{:S(2)}) copy-start(bf16[1024,256]{1,0:T(8,128)(2,1)} %add_convert_fusion.1) | copy-start | bytes 1572868
  (6 other events, 15.2 us)
Sparse Core Ops, SparseCore 0:
  9.1 53.9 all-gather.2
  196.7 45.3 reduce-scatter.2
  244.2 52.1 all-gather.4
  311.4 49.0 reduce-scatter.4
